TPU v7x, 128 devices: a whole 4x4x4 slice. The times are simulated.
128 devices in a mesh: grp: 32 (over z, y, core), head: 4 (over x).
Axes of the slice: x: 4, y: 4, z: 4, core: 2. Of those that a mesh axis runs over, the one named last changes fastest.
Arguments:
- activations: bfloat16 [1024, 4096], P('grp', 'head'), may hold values from -1.5 to 1.5
- ln_gain: bfloat16 [4096], replicated, may hold values from 0.099609375 to 1.8984375
- ln_bias: bfloat16 [4096], replicated, may hold values from -3 to 3
- w_qkv: bfloat16 [4096, 3, 4096], P('grp', None, 'head'), may hold values from -0.09375 to 0.09375
- prefix_keys: bfloat16 [64, 1024, 4096], P('grp', None, 'head')
- prefix_values: bfloat16 [64, 1024, 4096], P('grp', None, 'head'), may hold values from -6 to 6
- own_keys: bfloat16 [1024, 32, 4096], P('grp', None, 'head'), may hold values from -6 to 6
- own_values: bfloat16 [1024, 32, 4096], P('grp', None, 'head'), may hold values from -6 to 6
- prompt_len: int32 [64], P('grp'), may hold values from 64 to 1024, as said below
- own_len: int32 [1024], P('grp'), may hold values from 1 to 32, as said below
- w_attn_out: bfloat16 [256, 16, 4096], P('grp', 'head'), may hold values from -0.09375 to 0.09375
- w_in: bfloat16 [4096, 16384], P(None, ('grp', 'head')), may hold values from -0.09375 to 0.09375
- b_in: bfloat16 [16384], P(('grp', 'head')), may hold values from -4 to 4
- w_down: bfloat16 [16384, 4096], P(('grp', 'head')), may hold values from -0.046875 to 0.046875
- b_down: bfloat16 [4096], P('head'), may hold values from -3 to 3
Outputs:
- layer_out: bfloat16 [1024, 4096], P('grp', 'head')
Inputs may be any that keep to these rules, and one draw needn't show every extreme that they name: `prompt_len`: some group's prompt has exactly 1024 tokens and some has 64. `own_len`: some request has exactly 32 own tokens.
All inputs are finite; a program needn't handle non-finite values.
Results may differ from a plain program's by a relative error of at most 0.034.
Values may be sent and summed in bfloat16 or wider, within the bound.
No kernel may reach another device: no remote copies, remote signals or barrier semaphores. Data moves between devices by JAX's collectives and lax.ppermute only.
A program may use at most 128 MiB of HBM per device.

v0:
```python
import math
import jax
import jax.numpy as jnp
from jax import lax
from jax.sharding import PartitionSpec as P

HS = 256
ROT = 64
GSIZE = 16


def normalize(rows, gain, shift):
    floats = rows.astype(jnp.float32)
    center = floats - jnp.mean(floats, axis=-1, keepdims=True)
    spread = jnp.mean(center * center, axis=-1, keepdims=True)
    return (
        center * lax.rsqrt(spread + 1e-05) * gain.astype(jnp.float32) + shift.astype(jnp.float32)
    ).astype(jnp.bfloat16)


def rotate(values, positions):
    half = ROT // 2
    index = jnp.arange(half, dtype=jnp.float32)
    freqs = jnp.power(jnp.float32(10000.0), -2.0 * index / ROT)
    angle = positions[:, None, None] * freqs[None, None, :]
    cosine = jnp.cos(angle)
    sine = jnp.sin(angle)
    pairs = values[..., :ROT].reshape(values.shape[:-1] + (half, 2))
    first = pairs[..., 0]
    second = pairs[..., 1]
    turned = jnp.stack([first * cosine - second * sine, second * cosine + first * sine], axis=-1)
    turned = turned.reshape(values.shape[:-1] + (ROT,))
    return jnp.concatenate([turned, values[..., ROT:]], axis=-1)


def head_exchange(pieces, axis):
    count = lax.axis_size("head")
    here = lax.axis_index("head")
    received = []
    for shift in range(count):
        piece = lax.dynamic_index_in_dim(pieces, (here + shift) % count, axis, keepdims=False)
        if shift:
            piece = lax.ppermute(piece, "head", [(i, (i + shift) % count) for i in range(count)])
        received.append(piece)
    stacked = jnp.stack(received, axis=0)
    return jnp.take(stacked, (here - jnp.arange(count)) % count, axis=0)


def head_gather(piece):
    count = lax.axis_size("head")
    here = lax.axis_index("head")
    received = [piece]
    for shift in range(1, count):
        received.append(
            lax.ppermute(piece, "head", [(i, (i + shift) % count) for i in range(count)])
        )
    stacked = jnp.stack(received, axis=0)
    return jnp.take(stacked, (here - jnp.arange(count)) % count, axis=0)


def local(
    activations,
    ln_gain,
    ln_bias,
    w_qkv,
    prefix_keys,
    prefix_values,
    own_keys,
    own_values,
    prompt_len,
    own_len,
    w_attn_out,
    w_in,
    b_in,
    w_down,
    b_down,
):
    grp_count = lax.axis_size("grp")
    head_count = lax.axis_size("head")
    width_here = activations.shape[1]
    full_rows = jnp.moveaxis(head_gather(activations), 0, 1).reshape(activations.shape[0], -1)
    normed = normalize(full_rows, ln_gain, ln_bias)
    local_rows = normed.shape[0]
    groups_here = prompt_len.shape[0]
    gathered = lax.all_gather(normed, "grp", axis=0, tiled=True)
    block = w_qkv.shape[0]
    pair_rows = normed.reshape(local_rows, grp_count // 2, 2 * block)
    columns = lax.all_to_all(
        jnp.repeat(pair_rows, 2, axis=1), "grp", split_axis=1, concat_axis=0, tiled=True
    ).reshape(grp_count * local_rows, 2 * block)
    parity = lax.axis_index("grp") % 2
    half = w_qkv.shape[2] // 2
    own = lax.dynamic_slice_in_dim(w_qkv, parity * half, half, axis=2)
    other = lax.dynamic_slice_in_dim(w_qkv, (1 - parity) * half, half, axis=2)
    sibling = lax.ppermute(other, "grp", [(i, i ^ 1) for i in range(grp_count)])
    pair_weights = jnp.where(
        parity == 0,
        jnp.concatenate([own, sibling], axis=0),
        jnp.concatenate([sibling, own], axis=0),
    )
    term = jnp.einsum(
        "rf,fch->rch", columns, pair_weights, preferred_element_type=jnp.float32
    ).astype(jnp.bfloat16)
    received = lax.all_to_all(
        term.reshape(grp_count, local_rows, 3, half), "grp", 0, 0, tiled=True
    ).reshape(grp_count // 2, 2, local_rows, 3, half)
    qkv = jnp.sum(received.astype(jnp.float32), axis=0)
    qkv = jnp.transpose(qkv, (1, 2, 0, 3)).reshape(local_rows, 3, 2 * half)
    heads_here = w_qkv.shape[2] // HS
    member = (jnp.arange(local_rows) // GSIZE)[:, None] == jnp.arange(groups_here)[None, :]
    row_prompt = jnp.sum(jnp.where(member, prompt_len[None, :], 0), axis=1)
    positions = (row_prompt + own_len).astype(jnp.float32)
    query = rotate(qkv[:, 0].reshape(local_rows, heads_here, HS), positions).astype(jnp.bfloat16)
    key_new = rotate(qkv[:, 1].reshape(local_rows, heads_here, HS), positions).astype(jnp.bfloat16)
    value_new = qkv[:, 2].reshape(local_rows, heads_here, HS).astype(jnp.bfloat16)
    scale = 1.0 / math.sqrt(HS)
    longest = prefix_keys.shape[1]
    own_count = own_keys.shape[1]
    grouped = query.reshape(groups_here, GSIZE, heads_here, HS)
    pre_keys = prefix_keys.reshape(groups_here, longest, heads_here, HS)
    pre_vals = prefix_values.reshape(groups_here, longest, heads_here, HS)
    mine_keys = own_keys.reshape(local_rows, own_count, heads_here, HS)
    mine_vals = own_values.reshape(local_rows, own_count, heads_here, HS)
    pre_scores = (
        jnp.einsum("gqhd,gjhd->gqhj", grouped, pre_keys, preferred_element_type=jnp.float32) * scale
    )
    pre_scores = jnp.where(
        jnp.arange(longest)[None, None, None, :] < prompt_len[:, None, None, None],
        pre_scores,
        -jnp.inf,
    )
    own_scores = (
        jnp.einsum("rhd,rthd->rht", query, mine_keys, preferred_element_type=jnp.float32) * scale
    )
    own_scores = jnp.where(
        jnp.arange(own_count)[None, None, :] < own_len[:, None, None], own_scores, -jnp.inf
    )
    self_scores = (
        jnp.einsum("rhd,rhd->rh", query, key_new, preferred_element_type=jnp.float32) * scale
    )
    pre_peak = jnp.max(pre_scores, axis=-1).reshape(local_rows, heads_here)
    peak = jnp.maximum(jnp.maximum(pre_peak, jnp.max(own_scores, axis=-1)), self_scores)
    pre_exp = jnp.exp(pre_scores - peak.reshape(groups_here, GSIZE, heads_here)[..., None])
    own_exp = jnp.exp(own_scores - peak[..., None])
    self_exp = jnp.exp(self_scores - peak)
    denom = (
        jnp.sum(pre_exp, axis=-1).reshape(local_rows, heads_here)
        + jnp.sum(own_exp, axis=-1)
        + self_exp
    )
    mixed = jnp.einsum(
        "gqhj,gjhd->gqhd",
        pre_exp.astype(jnp.bfloat16),
        pre_vals,
        preferred_element_type=jnp.float32,
    )
    mixed = mixed.reshape(local_rows, heads_here, HS)
    mixed = mixed + jnp.einsum(
        "rht,rthd->rhd", own_exp.astype(jnp.bfloat16), mine_vals, preferred_element_type=jnp.float32
    )
    mixed = mixed + self_exp.astype(jnp.bfloat16).astype(jnp.float32)[..., None] * value_new.astype(
        jnp.float32
    )
    attended = (mixed / denom[..., None]).astype(jnp.bfloat16)
    dim_here = HS // grp_count
    outgoing = jnp.broadcast_to(
        jnp.transpose(attended.reshape(local_rows, heads_here, grp_count, dim_here), (2, 0, 1, 3))[
            :, None
        ],
        (grp_count, head_count, local_rows, heads_here, dim_here),
    ).reshape(grp_count * head_count, local_rows, heads_here, dim_here)
    incoming = lax.all_to_all(outgoing, ("grp", "head"), 0, 0, tiled=True).reshape(
        grp_count, head_count, local_rows, heads_here, dim_here
    )
    slices = jnp.transpose(incoming, (4, 1, 3, 0, 2)).reshape(
        dim_here, head_count * heads_here, grp_count * local_rows
    )
    out_blocks = head_exchange(w_attn_out.reshape(dim_here, heads_here, head_count, width_here), 2)
    out_blocks = jnp.moveaxis(out_blocks, 0, 1).reshape(
        dim_here, heads_here * head_count, width_here
    )
    units = w_in.shape[1]
    down_blocks = head_exchange(w_down.reshape(units, head_count, width_here), 1).reshape(
        units * head_count, width_here
    )
    hidden = jax.nn.gelu(
        jnp.dot(gathered, w_in, preferred_element_type=jnp.float32) + b_in.astype(jnp.float32),
        approximate=True,
    ).astype(jnp.bfloat16)
    hidden = lax.all_gather(hidden, "head", axis=1, tiled=True)
    mlp_part = jnp.dot(hidden, down_blocks, preferred_element_type=jnp.float32)
    attn_part = jnp.einsum("dkr,dkf->rf", slices, out_blocks, preferred_element_type=jnp.float32)
    combined = mlp_part + attn_part
    half_width = width_here // 2
    mine = lax.dynamic_slice_in_dim(combined, parity * half_width, half_width, axis=1)
    theirs = lax.dynamic_slice_in_dim(combined, (1 - parity) * half_width, half_width, axis=1)
    got = lax.ppermute(theirs.astype(jnp.bfloat16), "grp", [(i, i ^ 1) for i in range(grp_count)])
    pair_sum = (mine + got.astype(jnp.float32)).astype(jnp.bfloat16)
    pieces = lax.all_to_all(
        pair_sum.reshape(grp_count, local_rows, half_width), "grp", 0, 0, tiled=True
    ).reshape(grp_count // 2, 2, local_rows, half_width)
    summed = jnp.sum(pieces.astype(jnp.float32), axis=0)
    summed = jnp.transpose(summed, (1, 0, 2)).reshape(local_rows, width_here)
    total = activations.astype(jnp.float32) + b_down.astype(jnp.float32)[None, :] + summed
    return total.astype(jnp.bfloat16)


def solution(mesh):
    in_specs = (
        P("grp", "head"),
        P(),
        P(),
        P("grp", None, "head"),
        P("grp", None, "head"),
        P("grp", None, "head"),
        P("grp", None, "head"),
        P("grp", None, "head"),
        P("grp"),
        P("grp"),
        P("grp", "head", None),
        P(None, ("grp", "head")),
        P(("grp", "head")),
        P(("grp", "head"), None),
        P("head"),
    )
    out_specs = P("grp", "head")
    return jax.shard_map(local, mesh=mesh, in_specs=in_specs, out_specs=out_specs, check_vma=False)
```

profile of v0, /device:TPU:1, one launch (start us, length us, event | category | flops | bytes accessed | tf_op | source)
XLA Modules:
  0.0 190.7 jit_solution(12100319529735048736)
XLA Ops:
  6.5 2.1 %collective-permute-start = (bf16[32,1024]{1,0:T(8,128)(2,1)}, bf16[32,1024]{1,0:T(8,128)(2,1)S(1)}, u32[]{:S(2)}, u32[]{:S(2)}) collective-permute-start(bf16[32,1024]{1,0:T(8,128)(2,1)} %param.15), channel_id=1, source_target_pairs={{0,1},{1,2},{2,3},{3,0},{4,5},{5,6},{6,7},{7,4},{8,9},{9,10},{10,1... | collective-permute-start | bytes 196616 | tf_op jit(solution)/shard_map/ppermute | solution.py:55
  8.6 1.4 collective-permute-start.2
  10.0 1.6 collective-permute-start.1
  11.7 0.7 convert_element_type.107
  12.4 0.7 convert_element_type.108
  13.1 1.7 collective-permute-done.1
  14.8 0.9 pad_maximum_fusion.1
  15.7 0.6 gather_fusion
  16.7 0.3 fusion.39
  17.0 0.9 add_convert_fusion.2
  18.0 0.3 copy.132
  18.4 0.3 reshape.340
  18.9 0.9 broadcast_in_dim.106
  19.8 10.6 %all-to-all-start = ((bf16[32,32,256]{2,0,1:T(8,128)(2,1)}), bf16[32,32,256]{2,0,1:T(8,128)(2,1)S(1)}, u32[]{:S(2)}, u32[]{:S(2)}) async-start(bf16[32,32,256]{2,0,1:T(8,128)(2,1)} %bitcast.16), calls=%async_computation | async-start | bytes 1048576 | tf_op jit(solution)/shard_map/all_to_all | solution.py:88
  30.5 0.3 collective-permute-start.6
  30.8 1.5 collective-permute-done.6
  32.3 12.1 %all-to-all-done = bf16[32,32,256]{2,0,1:T(8,128)(2,1)S(1)} async-done(((bf16[32,32,256]{2,0,1:T(8,128)(2,1)}), bf16[32,32,256]{2,0,1:T(8,128)(2,1)S(1)}, u32[]{:S(2)}, u32[]{:S(2)}) %all-to-all-start) | async-done | bytes 524320 | tf_op jit(solution)/shard_map/all_to_all | solution.py:88
  44.5 1.0 convolution_convert_fusion
  45.5 2.1 %copy.140 = bf16[32,32,3,512]{3,1,2,0:T(8,128)(2,1)} copy(bf16[32,32,3,512]{3,1,0,2:T(8,128)(2,1)S(1)} %bitcast.166) | data formatting | bytes 6291456 | tf_op jit(solution)/shard_map/reshape | solution.py:105
  47.6 4.9 %all-to-all-start.1 = ((bf16[32,32,3,512]{3,1,2,0:T(8,128)(2,1)}), bf16[32,32,3,512]{3,1,2,0:T(8,128)(2,1)}, u32[]{:S(2)}, u32[]{:S(2)}) async-start(bf16[32,32,3,512]{3,1,2,0:T(8,128)(2,1)} %copy.140), calls=%async_computation.1 | async-start | bytes 6291456 | tf_op jit(solution)/shard_map/all_to_all | solution.py:104
  52.9 0.6 constant_dynamic-slice_fusion.3
  53.6 0.7 copy.261
  54.3 0.9 collective-permute-start.9
  55.2 0.7 copy.263
  55.9 0.6 collective-permute-start.7
  56.5 0.7 copy.262
  57.2 1.2 collective-permute-start.8
  58.3 0.7 copy.133
  59.2 1.6 collective-permute-start.3
  61.0 1.0 collective-permute-start.4
  62.1 0.7 iota_compare_fusion
  62.7 0.7 iota_compare_fusion.1
  63.4 0.7 multiply_cosine_fusion
  64.1 1.2 broadcast_bitcast_fusion
  65.3 1.2 convert_element_type.110
  66.9 1.8 collective-permute-start.5
  68.6 0.9 pad_maximum_fusion.2
  69.6 0.7 gather_fusion.2
  70.3 1.4 broadcast_select_fusion
  71.7 2.6 %collective-permute-done.4 = bf16[128,1024]{1,0:T(8,128)(2,1)} collective-permute-done((bf16[128,1024]{1,0:T(8,128)(2,1)S(1)}, bf16[128,1024]{1,0:T(8,128)(2,1)}, u32[]{:S(2)}, u32[]{:S(2)}) %collective-permute-start.4) | collective-permute-done | bytes 262176 | tf_op jit(solution)/shard_map/ppermute | solution.py:43
  74.3 0.7 copy-done.7
  75.0 1.2 pad_maximum_fusion
  76.2 0.7 gather_fusion.1
  76.9 32.3 %all-to-all-done.1 = bf16[32,32,3,512]{3,1,2,0:T(8,128)(2,1)} async-done(((bf16[32,32,3,512]{3,1,2,0:T(8,128)(2,1)}), bf16[32,32,3,512]{3,1,2,0:T(8,128)(2,1)}, u32[]{:S(2)}, u32[]{:S(2)}) %all-to-all-start.1) | async-done | bytes 3145760 | tf_op jit(solution)/shard_map/all_to_all | solution.py:104
  109.3 2.5 %convert_reduce_fusion = f32[2,32,3,512]{3,1,2,0:T(8,128)S(1)} fusion(bf16[16,2,32,3,512]{4,2,3,1,0:T(8,128)(2,1)} %bitcast.53), kind=kLoop, calls=%fused_computation.3 | loop fusion | flops 3047424 | bytes 3538944 | tf_op jit(solution)/shard_map/reduce_sum | solution.py:107
  114.2 3.5 %fusion.68 = (f32[2,16,4]{1,2,0:T(4,128)S(1)}, f32[2,16,4,1024]{3,1,2,0:T(8,128)S(1)}) fusion(bf16[2,128,4,8,256]{4,3,2,1,0:T(8,128)(2,1)} %bitcast.161, bf16[2,16,4,64]{3,1,2,0:T(8,128)(2,1)S(1)} %copy.145, pred[2,1024]{1,0:T(4,128)(4,1)S(1)} %copy-done.12, bf16[2,16,4,192]{3,1,0,2:T(8,128)(2,1)S(1)} %bitcast.173), kind=kOutput, calls=%fused_computation.142 | convolution fusion | flops 67633024 | bytes 4786688 | tf_op jit(solution)/shard_map/gqhd,gjhd->gqhj/dot_general | solution.py:125
  117.7 2.2 %fusion.9 = f32[32,4,1,32]{3,2,1,0:T(1,128)S(1)} fusion(bf16[32,4,4,8,256]{4,3,2,1,0:T(8,128)(2,1)} %bitcast.192, bf16[32,4,256,1]{2,0,1,3:T(8,128)(2,1)S(1)} %get-tuple-element.25), kind=kOutput, calls=%fused_computation.15 | convolution fusion | flops 2097152 | bytes 2179072 | tf_op jit(solution)/shard_map/rhd,rthd->rht/dot_general | solution.py:133
  120.2 6.5 %fusion.37 = bf16[1024,128]{1,0:T(8,128)(2,1)} fusion(bf16[1024,4096]{1,0:T(8,128)(2,1)} %all-gather.3.cloned.1.call-done, bf16[4096,128]{1,0:T(8,128)(2,1)S(1)} %copy-done, f32[128]{0:T(128)S(1)} %copy-done.19), kind=kOutput, calls=%fused_computation.47 | convolution fusion | flops 1075052544 | bytes 9699840 | tf_op jit(solution)/shard_map/dot_general | solution.py:187
  126.7 2.9 %fusion.21 = f32[2,16,4,256]{3,1,2,0:T(8,128)S(1)} fusion(bf16[2,128,4,8,256]{4,3,2,1,0:T(8,128)(2,1)} %bitcast.164, f32[2,16,4,1024]{3,1,2,0:T(8,128)S(1)} %get-tuple-element.32, f32[2,16,4]{1,2,0:T(4,128)S(1)} %copy.152), kind=kOutput, calls=%fused_computation.25 | convolution fusion | flops 67371008 | bytes 4850176 | tf_op jit(solution)/shard_map/gqhj,gjhd->gqhd/dot_general | solution.py:151
  130.1 2.0 %fusion.6 = f32[32,4,1,256]{3,2,1,0:T(1,128)S(1)} fusion(bf16[32,4,4,8,256]{4,3,2,1,0:T(8,128)(2,1)} %bitcast.193, bf16[32,4,32,1]{2,0,1,3:T(8,128)(2,1)S(1)} %get-tuple-element.28), kind=kOutput, calls=%fused_computation.12 | convolution fusion | flops 2097152 | bytes 2236416 | tf_op jit(solution)/shard_map/rht,rthd->rhd/dot_general | solution.py:158
  132.7 1.5 reshape.381
  134.2 4.1 %all-to-all-start.2 = ((bf16[128,2,512]{2,1,0:T(2,128)(2,1)}), bf16[128,2,512]{2,1,0:T(2,128)(2,1)S(1)}, u32[]{:S(2)}, u32[]{:S(2)}) async-start(bf16[128,2,512]{2,1,0:T(2,128)(2,1)} %reshape.381), calls=%async_computation.2 | async-start | bytes 524288 | tf_op jit(solution)/shard_map/all_to_all | solution.py:172
  138.5 12.8 %all-to-all-done.2 = bf16[128,2,512]{2,1,0:T(2,128)(2,1)S(1)} async-done(((bf16[128,2,512]{2,1,0:T(2,128)(2,1)}), bf16[128,2,512]{2,1,0:T(2,128)(2,1)S(1)}, u32[]{:S(2)}, u32[]{:S(2)}) %all-to-all-start.2) | async-done | bytes 262176 | tf_op jit(solution)/shard_map/all_to_all | solution.py:172
  151.3 0.5 reshape.382
  151.8 0.7 copy.159
  152.5 1.1 reshape.334
  153.6 2.5 %fusion.69 = f32[1024,1024]{1,0:T(8,128)S(1)} fusion(bf16[1024,512]{1,0:T(8,128)(2,1)} %all-gather.5.cloned.1.call-done, bf16[512,1024]{1,0:T(8,128)(2,1)S(1)} %bitcast_select_fusion), kind=kOutput, calls=%fused_computation.143 | convolution fusion | flops 1073741824 | bytes 6291456 | tf_op jit(solution)/shard_map/dot_general | solution.py:191
  156.1 0.8 bitcast_add_fusion
  157.1 0.5 collective-permute-start.10
  157.6 2.3 %collective-permute-done.10 = bf16[1024,512]{1,0:T(8,128)(2,1)S(1)} collective-permute-done((bf16[1024,512]{1,0:T(8,128)(2,1)S(1)}, bf16[1024,512]{1,0:T(8,128)(2,1)S(1)}, u32[]{:S(2)}, u32[]{:S(2)}) %collective-permute-start.10) | collective-permute-done | bytes 1048608 | tf_op jit(solution)/shard_map/ppermute | solution.py:197
  159.9 1.4 add_convert_fusion
  161.3 4.7 %all-to-all-start.3 = ((bf16[32,32,512]{2,1,0:T(8,128)(2,1)}), bf16[32,32,512]{2,1,0:T(8,128)(2,1)S(1)}, u32[]{:S(2)}, u32[]{:S(2)}) async-start(bf16[32,32,512]{2,1,0:T(8,128)(2,1)} %bitcast.47), calls=%async_computation.3 | async-start | bytes 2097152 | tf_op jit(solution)/shard_map/all_to_all | solution.py:199
  166.0 17.0 %all-to-all-done.3 = bf16[32,32,512]{2,1,0:T(8,128)(2,1)S(1)} async-done(((bf16[32,32,512]{2,1,0:T(8,128)(2,1)}), bf16[32,32,512]{2,1,0:T(8,128)(2,1)S(1)}, u32[]{:S(2)}, u32[]{:S(2)}) %all-to-all-start.3) | async-done | bytes 1048608 | tf_op jit(solution)/shard_map/all_to_all | solution.py:199
  183.2 0.7 add_convert_fusion.3
  (121 shorter events, 6.1 us)
Async XLA Ops:
  6.5 113.7 %copy-start = (bf16[4096,128]{1,0:T(8,128)(2,1)S(1)}, bf16[4096,128]{1,0:T(8,128)(2,1)}, u32[]{:S(2)}) copy-start(bf16[4096,128]{1,0:T(8,128)(2,1)} %param.26) | copy-start | bytes 3145732
  6.5 11.4 %copy-start.10 = (bf16[4096]{0:T(1024)(128)(2,1)S(1)}, bf16[4096]{0:T(1024)(128)(2,1)}, u32[]{:S(2)}) copy-start(bf16[4096]{0:T(1024)(128)(2,1)} %param.16) | copy-start | bytes 24580
  6.5 11.4 %copy-start.11 = (bf16[4096]{0:T(1024)(128)(2,1)S(1)}, bf16[4096]{0:T(1024)(128)(2,1)}, u32[]{:S(2)}) copy-start(bf16[4096]{0:T(1024)(128)(2,1)} %param.17) | copy-start | bytes 24580
  6.5 113.7 %all-gather.3.cloned.1.call-start = ((), (), s32[]{:S(2)}) async-start(), calls=%async_computation.4 | async-start | bytes 8650752 | tf_op jit(solution)/shard_map/all_gather | solution.py:85
  6.5 6.6 %collective-permute-start = (bf16[32,1024]{1,0:T(8,128)(2,1)}, bf16[32,1024]{1,0:T(8,128)(2,1)S(1)}, u32[]{:S(2)}, u32[]{:S(2)}) collective-permute-start(bf16[32,1024]{1,0:T(8,128)(2,1)} %param.15), channel_id=1, source_target_pairs={{0,1},{1,2},{2,3},{3,0},{4,5},{5,6},{6,7},{7,4},{8,9},{9,10},{10,1... | collective-permute-start | bytes 196616 | tf_op jit(solution)/shard_map/ppermute | solution.py:55
  8.6 4.5 %collective-permute-start.2 = (bf16[32,1024]{1,0:T(8,128)(2,1)}, bf16[32,1024]{1,0:T(8,128)(2,1)S(1)}, u32[]{:S(2)}, u32[]{:S(2)}) collective-permute-start(bf16[32,1024]{1,0:T(8,128)(2,1)} %param.15), channel_id=1, source_target_pairs={{0,3},{1,0},{2,1},{3,2},{4,7},{5,4},{6,5},{7,6},{8,11},{9,8},{10,9... | collective-permute-start | bytes 196616 | tf_op jit(solution)/shard_map/ppermute | solution.py:55
  10.0 4.8 %collective-permute-start.1 = (bf16[32,1024]{1,0:T(8,128)(2,1)}, bf16[32,1024]{1,0:T(8,128)(2,1)S(1)}, u32[]{:S(2)}, u32[]{:S(2)}) collective-permute-start(bf16[32,1024]{1,0:T(8,128)(2,1)} %param.15), channel_id=1, source_target_pairs={{0,2},{1,3},{2,0},{3,1},{4,6},{5,7},{6,4},{7,5},{8,10},{9,11},{10,... | collective-permute-start | bytes 196616 | tf_op jit(solution)/shard_map/ppermute | solution.py:55
  11.7 4.6 %copy-start.14 = (s32[1024]{0:T(1024)}, s32[1024]{0:T(1024)S(1)}, u32[]{:S(2)}) copy-start(s32[1024]{0:T(1024)S(1)} %pad_clamp_fusion) | copy-start | bytes 12292
  13.1 4.9 %copy-start.13 = (pred[4]{0:T(512)(128)(4,1)}, pred[4]{0:T(512)(128)(4,1)S(1)}, u32[]{:S(2)}) copy-start(pred[4]{0:T(512)(128)(4,1)S(1)} %compare_and_fusion) | copy-start | bytes 16
  17.0 13.4 %copy-start.3 = (bf16[128,3,1024]{2,0,1:T(8,128)(2,1)S(1)}, bf16[128,3,1024]{2,0,1:T(8,128)(2,1)}, u32[]{:S(2)}) copy-start(bf16[128,3,1024]{2,0,1:T(8,128)(2,1)} %param.18) | copy-start | bytes 2359300
  19.8 24.6 %all-to-all-start = ((bf16[32,32,256]{2,0,1:T(8,128)(2,1)}), bf16[32,32,256]{2,0,1:T(8,128)(2,1)S(1)}, u32[]{:S(2)}, u32[]{:S(2)}) async-start(bf16[32,32,256]{2,0,1:T(8,128)(2,1)} %bitcast.16), calls=%async_computation | async-start | bytes 1048576 | tf_op jit(solution)/shard_map/all_to_all | solution.py:88
  30.5 1.8 collective-permute-start.6
  47.6 5.0 %copy-start.5 = (bf16[8,4,4096]{2,1,0:T(4,128)(2,1)S(1)}, bf16[8,4,4096]{2,1,0:T(4,128)(2,1)}, u32[]{:S(2)}) copy-start(bf16[8,4,4096]{2,1,0:T(4,128)(2,1)} %param.25) | copy-start | bytes 786436
  47.6 10.7 %copy-start.2 = (bf16[128,4096]{1,0:T(8,128)(2,1)S(1)}, bf16[128,4096]{1,0:T(8,128)(2,1)}, u32[]{:S(2)}) copy-start(bf16[128,4096]{1,0:T(8,128)(2,1)} %param.28) | copy-start | bytes 3145732
  47.6 61.6 %all-to-all-start.1 = ((bf16[32,32,3,512]{3,1,2,0:T(8,128)(2,1)}), bf16[32,32,3,512]{3,1,2,0:T(8,128)(2,1)}, u32[]{:S(2)}, u32[]{:S(2)}) async-start(bf16[32,32,3,512]{3,1,2,0:T(8,128)(2,1)} %copy.140), calls=%async_computation.1 | async-start | bytes 6291456 | tf_op jit(solution)/shard_map/all_to_all | solution.py:104
  52.6 101.0 %all-gather.5.cloned.1.call-start = ((), (), s32[]{:S(2)}) async-start(), calls=%async_computation.5 | async-start | bytes 1310720 | tf_op jit(solution)/shard_map/all_gather | solution.py:190
  53.6 8.4 %copy-start.18 = (s32[2]{0:T(128)S(1)}, s32[2]{0:T(128)}, u32[]{:S(2)}) copy-start(s32[2]{0:T(128)} %param.23) | copy-start | bytes 28
  53.6 8.5 %copy-start.17 = (s32[32]{0:T(128)S(1)}, s32[32]{0:T(128)}, u32[]{:S(2)}) copy-start(s32[32]{0:T(128)} %param.24) | copy-start | bytes 388
  54.3 12.6 %collective-permute-start.9 = (bf16[8,4,1024]{2,0,1:T(8,128)(2,1)}, bf16[8,4,1024]{2,0,1:T(8,128)(2,1)}, u32[]{:S(2)}, u32[]{:S(2)}) collective-permute-start(bf16[8,4,1024]{2,0,1:T(8,128)(2,1)} %bitcast.156), channel_id=1, source_target_pairs={{0,3},{1,0},{2,1},{3,2},{4,7},{5,4},{6,5},{7,6},{8,11},{9,8},{10,9... | collective-permute-start | bytes 196616 | tf_op jit(solution)/shard_map/ppermute | solution.py:43
  55.9 12.8 %collective-permute-start.7 = (bf16[8,4,1024]{2,0,1:T(8,128)(2,1)}, bf16[8,4,1024]{2,0,1:T(8,128)(2,1)}, u32[]{:S(2)}, u32[]{:S(2)}) collective-permute-start(bf16[8,4,1024]{2,0,1:T(8,128)(2,1)} %bitcast.158), channel_id=1, source_target_pairs={{0,1},{1,2},{2,3},{3,0},{4,5},{5,6},{6,7},{7,4},{8,9},{9,10},{10,1... | collective-permute-start | bytes 196616 | tf_op jit(solution)/shard_map/ppermute | solution.py:43
  57.2 11.5 %collective-permute-start.8 = (bf16[8,4,1024]{2,0,1:T(8,128)(2,1)}, bf16[8,4,1024]{2,0,1:T(8,128)(2,1)}, u32[]{:S(2)}, u32[]{:S(2)}) collective-permute-start(bf16[8,4,1024]{2,0,1:T(8,128)(2,1)} %bitcast.157), channel_id=1, source_target_pairs={{0,2},{1,3},{2,0},{3,1},{4,6},{5,7},{6,4},{7,5},{8,10},{9,11},{10,... | collective-permute-start | bytes 196616 | tf_op jit(solution)/shard_map/ppermute | solution.py:43
  59.2 12.5 %collective-permute-start.3 = (bf16[128,1024]{1,0:T(8,128)(2,1)S(1)}, bf16[128,1024]{1,0:T(8,128)(2,1)S(1)}, u32[]{:S(2)}, u32[]{:S(2)}) collective-permute-start(bf16[128,1024]{1,0:T(8,128)(2,1)S(1)} %bitcast.182), channel_id=1, source_target_pairs={{0,1},{1,2},{2,3},{3,0},{4,5},{5,6},{6,7},{7,4},{8,9},{9,10},{10,1... | collective-permute-start | bytes 786440 | tf_op jit(solution)/shard_map/ppermute | solution.py:43
  61.0 13.3 %collective-permute-start.4 = (bf16[128,1024]{1,0:T(8,128)(2,1)S(1)}, bf16[128,1024]{1,0:T(8,128)(2,1)}, u32[]{:S(2)}, u32[]{:S(2)}) collective-permute-start(bf16[128,1024]{1,0:T(8,128)(2,1)S(1)} %bitcast.183), channel_id=1, source_target_pairs={{0,2},{1,3},{2,0},{3,1},{4,6},{5,7},{6,4},{7,5},{8,10},{9,11},{10,... | collective-permute-start | bytes 786440 | tf_op jit(solution)/shard_map/ppermute | solution.py:43
  66.9 7.4 %collective-permute-start.5 = (bf16[128,1024]{1,0:T(8,128)(2,1)S(1)}, bf16[128,1024]{1,0:T(8,128)(2,1)S(1)}, u32[]{:S(2)}, u32[]{:S(2)}) collective-permute-start(bf16[128,1024]{1,0:T(8,128)(2,1)S(1)} %bitcast.184), channel_id=1, source_target_pairs={{0,3},{1,0},{2,1},{3,2},{4,7},{5,4},{6,5},{7,6},{8,11},{9,8},{10,9... | collective-permute-start | bytes 786440 | tf_op jit(solution)/shard_map/ppermute | solution.py:43
  74.3 0.7 copy-start.7
  109.3 3.2 %copy-start.8 = (f32[32,32]{0,1:T(8,128)S(1)}, f32[32,32]{0,1:T(8,128)}, u32[]{:S(2)}) copy-start(f32[32,32]{0,1:T(8,128)} %get-tuple-element.30) | copy-start | bytes 12292
  111.8 2.4 %copy-start.12 = (pred[2,1024]{1,0:T(4,128)(4,1)S(1)}, pred[2,1024]{1,0:T(4,128)(4,1)}, u32[]{:S(2)}) copy-start(pred[2,1024]{1,0:T(4,128)(4,1)} %iota_compare_fusion.1) | copy-start | bytes 6148
  114.2 5.8 %copy-start.9 = (pred[32,32]{1,0:T(8,128)(4,1)S(1)}, pred[32,32]{1,0:T(8,128)(4,1)}, u32[]{:S(2)}) copy-start(pred[32,32]{1,0:T(8,128)(4,1)} %iota_compare_fusion) | copy-start | bytes 3076
  114.2 6.0 %copy-start.19 = (f32[128]{0:T(128)S(1)}, f32[128]{0:T(128)}, u32[]{:S(2)}) copy-start(f32[128]{0:T(128)} %convert_element_type.110) | copy-start | bytes 1540
  130.1 8.1 %copy-start.16 = (pred[512]{0:T(512)(128)(4,1)S(1)}, pred[512]{0:T(512)(128)(4,1)}, u32[]{:S(2)}) copy-start(pred[512]{0:T(512)(128)(4,1)} %broadcast_bitcast_fusion) | copy-start | bytes 1540
  134.2 17.1 %all-to-all-start.2 = ((bf16[128,2,512]{2,1,0:T(2,128)(2,1)}), bf16[128,2,512]{2,1,0:T(2,128)(2,1)S(1)}, u32[]{:S(2)}, u32[]{:S(2)}) async-start(bf16[128,2,512]{2,1,0:T(2,128)(2,1)} %reshape.381), calls=%async_computation.2 | async-start | bytes 524288 | tf_op jit(solution)/shard_map/all_to_all | solution.py:172
  153.6 2.6 %copy-start.4 = (bf16[4,8,4,1024]{3,1,2,0:T(8,128)(2,1)S(1)}, bf16[4,8,4,1024]{3,1,2,0:T(8,128)(2,1)}, u32[]{:S(2)}) copy-start(bf16[4,8,4,1024]{3,1,2,0:T(8,128)(2,1)} %broadcast_select_fusion) | copy-start | bytes 786436
  156.9 26.9 %copy-start.1 = (bf16[4096,128]{1,0:T(8,128)(2,1)S(1)}, bf16[4096,128]{1,0:T(8,128)(2,1)}, u32[]{:S(2)}) copy-start(bf16[4096,128]{1,0:T(8,128)(2,1)} %param.26) | copy-start | bytes 3145732
  157.1 8.9 %copy-start.15 = (bf16[1024]{0:T(1024)(128)(2,1)S(1)}, bf16[1024]{0:T(1024)(128)(2,1)}, u32[]{:S(2)}) copy-start(bf16[1024]{0:T(1024)(128)(2,1)} %param.29) | copy-start | bytes 6148
  157.1 26.1 %copy-start.6 = (bf16[32,1024]{1,0:T(8,128)(2,1)S(1)}, bf16[32,1024]{1,0:T(8,128)(2,1)}, u32[]{:S(2)}) copy-start(bf16[32,1024]{1,0:T(8,128)(2,1)} %param.15) | copy-start | bytes 196612
  157.1 2.8 %collective-permute-start.10 = (bf16[1024,512]{1,0:T(8,128)(2,1)S(1)}, bf16[1024,512]{1,0:T(8,128)(2,1)S(1)}, u32[]{:S(2)}, u32[]{:S(2)}) collective-permute-start(bf16[1024,512]{1,0:T(8,128)(2,1)S(1)} %dynamic-slice_convert_fusion), channel_id=1, source_target_pairs={{0,4},{4,0},{8,12},{12,8},{16,20},{20,16},{24,28},{28,24},{32,36},... | collective-permute-start | bytes 3145736 | tf_op jit(solution)/shard_map/ppermute | solution.py:197
  161.3 21.7 %all-to-all-start.3 = ((bf16[32,32,512]{2,1,0:T(8,128)(2,1)}), bf16[32,32,512]{2,1,0:T(8,128)(2,1)S(1)}, u32[]{:S(2)}, u32[]{:S(2)}) async-start(bf16[32,32,512]{2,1,0:T(8,128)(2,1)} %bitcast.47), calls=%async_computation.3 | async-start | bytes 2097152 | tf_op jit(solution)/shard_map/all_to_all | solution.py:199
Sparse Core Ops, SparseCore 0:
  18.0 90.7 all-gather.2
  126.8 22.8 all-gather.4
where the time goes:
time: 192 us; the launch traced here: 191 us
  waiting for transfers between devices  82.4 us (43%)
  starting transfers between devices  37.1 us (19%)
  matrix products  21.4 us (11%)
  local copies, waits for them, and re-layouts  18 us (9%)
  other arithmetic  17.4 us (9%)
  between operations  14.3 us (7%)
    all_to_all x1, waiting for transfers between devices, local(): lax.all_to_all(term.reshape(grp_count, local_rows, 3, half), 'grp', 0, 0,...  32.3 us
    all_to_all x1, waiting for transfers between devices, local(): lax.all_to_all(pair_sum.reshape(grp_count, local_rows, half_width), 'grp'...  17 us
    all_to_all x1, waiting for transfers between devices, local(): lax.all_to_all(outgoing, ('grp', 'head'), 0, 0, tiled=True)  12.8 us
    all_to_all x1, waiting for transfers between devices, local(): lax.all_to_all(jnp.repeat(pair_rows, 2, axis=1), 'grp', split_axis=1, con...  12.1 us
    all_to_all x1, starting transfers between devices, local(): lax.all_to_all(jnp.repeat(pair_rows, 2, axis=1), 'grp', split_axis=1, con...  10.6 us
    ppermute x6, starting transfers between devices, head_exchange(): lax.ppermute(piece, 'head', [(i, (i + shift) % count) for i in range(coun...  6.95 us
    dot_general x1, matrix products, local(): jnp.dot(gathered, w_in, preferred_element_type=jnp.float32)  6.47 us
    unnamed x50, local copies, waits for them, and re-layouts  5.88 us
  transfers between devices with their start and end apart: 17, of which 8 were waited for; matrix products, arithmetic and copies ran while one was open for 21% of the time, Pallas kernels for 0%

commit v1 on v0

--- a/solution.py
+++ b/solution.py
@@ -85,8 +85,14 @@
     gathered = lax.all_gather(normed, "grp", axis=0, tiled=True)
     block = w_qkv.shape[0]
     pair_rows = normed.reshape(local_rows, grp_count // 2, 2 * block)
-    columns = lax.all_to_all(
-        jnp.repeat(pair_rows, 2, axis=1), "grp", split_axis=1, concat_axis=0, tiled=True
+    columns = jnp.concatenate(
+        lax.all_to_all(
+            jnp.stack(jnp.split(jnp.repeat(pair_rows, 2, axis=1), lax.axis_size("grp"), axis=1)),
+            axis_name="grp",
+            split_axis=0,
+            concat_axis=0,
+        ),
+        axis=0,
     ).reshape(grp_count * local_rows, 2 * block)
     parity = lax.axis_index("grp") % 2
     half = w_qkv.shape[2] // 2

time: 192 us -> 195 us (1.016)
  waiting for transfers between devices: 82.4 us -> 64.1 us
  local copies, waits for them, and re-layouts: 18 us -> 36.3 us
  starting transfers between devices: 37.1 us -> 40.2 us
    unnamed x50 -> x81, local copies, waits for them, and re-layouts: 5.88 us -> 24.5 us
    all_to_all x1, waiting for transfers between devices: 32.3 us -> 14.3 us  [local(): lax.all_to_all(term.reshape(grp_count, local_rows, 3, half), 'grp', 0, 0,...]
    all_to_all x1, starting transfers between devices: 4.06 us -> 7.16 us  [local(): lax.all_to_all(outgoing, ('grp', 'head'), 0, 0, tiled=True)]
  transfers between devices with their start and end apart: 17 -> 17, of which waited for: 8 -> 8; matrix products, arithmetic and copies ran while one was open for 21% -> 31% of each run, Pallas kernels for 0% -> 0%
where the time goes in v1:
time: 195 us; the launch traced here: 194 us
  waiting for transfers between devices  64.1 us (33%)
  starting transfers between devices  40.2 us (21%)
  local copies, waits for them, and re-layouts  36.3 us (19%)
  matrix products  21.4 us (11%)
  other arithmetic  17.4 us (9%)
  between operations  14.3 us (7%)
    unnamed x81, local copies, waits for them, and re-layouts  24.5 us
    all_to_all x1, waiting for transfers between devices, local(): lax.all_to_all(pair_sum.reshape(grp_count, local_rows, half_width), 'grp'...  17 us
    all_to_all x1, waiting for transfers between devices, local(): lax.all_to_all(term.reshape(grp_count, local_rows, 3, half), 'grp', 0, 0,...  14.3 us
    all_to_all x1, waiting for transfers between devices, local(): lax.all_to_all(outgoing, ('grp', 'head'), 0, 0, tiled=True)  12.9 us
    all_to_all x1, waiting for transfers between devices, local(): lax.all_to_all(jnp.stack(jnp.split(jnp.repeat(pair_rows, 2, axis=1), lax....  11.8 us
    all_to_all x1, starting transfers between devices, local(): lax.all_to_all(jnp.stack(jnp.split(jnp.repeat(pair_rows, 2, axis=1), lax....  10.6 us
    all_to_all x1, starting transfers between devices, local(): lax.all_to_all(outgoing, ('grp', 'head'), 0, 0, tiled=True)  7.16 us
    ppermute x6, starting transfers between devices, head_exchange(): lax.ppermute(piece, 'head', [(i, (i + shift) % count) for i in range(coun...  6.9 us
  transfers between devices with their start and end apart: 17, of which 8 were waited for; matrix products, arithmetic and copies ran while one was open for 31% of the time, Pallas kernels for 0%

profile of v1, /device:TPU:1, one launch (start us, length us, event | category | flops | bytes accessed | tf_op | source)
XLA Modules:
  0.0 193.7 jit_solution(17578902579738434299)
XLA Ops:
  6.5 2.1 %collective-permute-start = (bf16[32,1024]{1,0:T(8,128)(2,1)}, bf16[32,1024]{1,0:T(8,128)(2,1)S(1)}, u32[]{:S(2)}, u32[]{:S(2)}) collective-permute-start(bf16[32,1024]{1,0:T(8,128)(2,1)} %param.15), channel_id=1, source_target_pairs={{0,1},{1,2},{2,3},{3,0},{4,5},{5,6},{6,7},{7,4},{8,9},{9,10},{10,1... | collective-permute-start | bytes 196616 | tf_op jit(solution)/shard_map/ppermute | solution.py:55
  8.6 1.4 collective-permute-start.2
  10.0 1.6 collective-permute-start.1
  11.7 0.7 convert_element_type.107
  12.4 0.7 convert_element_type.108
  13.1 1.7 collective-permute-done.1
  14.8 0.9 pad_maximum_fusion.1
  17.0 0.9 add_convert_fusion.2
  19.0 0.6 constant_dynamic-update-slice_fusion.31
  22.6 0.6 constant_dynamic-update-slice_fusion.25
  23.2 0.6 constant_dynamic-update-slice_fusion.24
  25.0 0.6 constant_dynamic-update-slice_fusion.21
  28.6 0.6 constant_dynamic-update-slice_fusion.15
  29.8 0.6 constant_dynamic-update-slice_fusion.13
  30.4 0.6 constant_dynamic-update-slice_fusion.12
  32.8 0.6 constant_dynamic-update-slice_fusion.8
  35.2 0.6 constant_dynamic-update-slice_fusion.4
  37.0 0.6 constant_dynamic-update-slice_fusion.1
  38.2 10.6 %all-to-all-start = ((bf16[32,32,1,256]{3,1,2,0:T(8,128)(2,1)}), bf16[32,32,1,256]{3,1,2,0:T(8,128)(2,1)S(1)}, u32[]{:S(2)}, u32[]{:S(2)}) async-start(bf16[32,32,1,256]{3,1,2,0:T(8,128)(2,1)} %constant_dynamic-update-slice_fusion), calls=%async_computation | async-start | bytes 1048576 | tf_op jit(solution)/shard_map/all_to_all | solution.py:89
  49.2 1.5 collective-permute-done.6
  50.7 11.8 %all-to-all-done = bf16[32,32,1,256]{3,1,2,0:T(8,128)(2,1)S(1)} async-done(((bf16[32,32,1,256]{3,1,2,0:T(8,128)(2,1)}), bf16[32,32,1,256]{3,1,2,0:T(8,128)(2,1)S(1)}, u32[]{:S(2)}, u32[]{:S(2)}) %all-to-all-start) | async-done | bytes 524320 | tf_op jit(solution)/shard_map/all_to_all | solution.py:89
  62.5 1.0 convolution_convert_fusion
  63.5 2.1 %copy.233 = bf16[32,32,3,512]{3,1,2,0:T(8,128)(2,1)} copy(bf16[32,32,3,512]{3,1,0,2:T(8,128)(2,1)S(1)} %bitcast.290) | data formatting | bytes 6291456 | tf_op jit(solution)/shard_map/reshape | solution.py:111
  65.6 5.1 %all-to-all-start.1 = ((bf16[32,32,3,512]{3,1,2,0:T(8,128)(2,1)}), bf16[32,32,3,512]{3,1,2,0:T(8,128)(2,1)}, u32[]{:S(2)}, u32[]{:S(2)}) async-start(bf16[32,32,3,512]{3,1,2,0:T(8,128)(2,1)} %copy.233), calls=%async_computation.1 | async-start | bytes 6291456 | tf_op jit(solution)/shard_map/all_to_all | solution.py:110
  71.1 0.6 constant_dynamic-slice_fusion.3
  71.8 0.7 copy.354
  72.6 0.7 copy.356
  73.3 1.3 collective-permute-start.7
  74.7 0.7 copy.355
  75.7 0.7 copy.226
  76.6 1.6 collective-permute-start.3
  78.4 1.7 collective-permute-start.4
  80.3 0.7 iota_compare_fusion
  80.9 0.7 iota_compare_fusion.1
  81.6 0.7 multiply_cosine_fusion
  82.3 1.2 broadcast_bitcast_fusion
  83.5 1.2 convert_element_type.110
  85.1 1.7 collective-permute-start.5
  86.8 0.9 pad_maximum_fusion.2
  87.8 0.7 gather_fusion.2
  88.4 1.4 broadcast_select_fusion
  89.9 2.6 %collective-permute-done.4 = bf16[128,1024]{1,0:T(8,128)(2,1)} collective-permute-done((bf16[128,1024]{1,0:T(8,128)(2,1)S(1)}, bf16[128,1024]{1,0:T(8,128)(2,1)}, u32[]{:S(2)}, u32[]{:S(2)}) %collective-permute-start.4) | collective-permute-done | bytes 262176 | tf_op jit(solution)/shard_map/ppermute | solution.py:43
  92.5 0.7 copy-done.7
  93.2 1.2 pad_maximum_fusion
  94.4 0.7 gather_fusion.1
  95.1 14.3 %all-to-all-done.1 = bf16[32,32,3,512]{3,1,2,0:T(8,128)(2,1)} async-done(((bf16[32,32,3,512]{3,1,2,0:T(8,128)(2,1)}), bf16[32,32,3,512]{3,1,2,0:T(8,128)(2,1)}, u32[]{:S(2)}, u32[]{:S(2)}) %all-to-all-start.1) | async-done | bytes 3145760 | tf_op jit(solution)/shard_map/all_to_all | solution.py:110
  109.4 2.5 %convert_reduce_fusion = f32[2,32,3,512]{3,1,2,0:T(8,128)S(1)} fusion(bf16[16,2,32,3,512]{4,2,3,1,0:T(8,128)(2,1)} %bitcast.81), kind=kLoop, calls=%fused_computation.3 | loop fusion | flops 3047424 | bytes 3538944 | tf_op jit(solution)/shard_map/reduce_sum | solution.py:113
  114.3 3.5 %fusion.68 = (f32[2,16,4]{1,2,0:T(4,128)S(1)}, f32[2,16,4,1024]{3,1,2,0:T(8,128)S(1)}) fusion(bf16[2,128,4,8,256]{4,3,2,1,0:T(8,128)(2,1)} %bitcast.285, bf16[2,16,4,64]{3,1,2,0:T(8,128)(2,1)S(1)} %copy.238, pred[2,1024]{1,0:T(4,128)(4,1)S(1)} %copy-done.12, bf16[2,16,4,192]{3,1,0,2:T(8,128)(2,1)S(1)} %bitcast.329), kind=kOutput, calls=%fused_computation.206 | convolution fusion | flops 67633024 | bytes 4786688 | tf_op jit(solution)/shard_map/gqhd,gjhd->gqhj/dot_general | solution.py:131
  117.8 2.2 %fusion.9 = f32[32,4,1,32]{3,2,1,0:T(1,128)S(1)} fusion(bf16[32,4,4,8,256]{4,3,2,1,0:T(8,128)(2,1)} %bitcast.348, bf16[32,4,256,1]{2,0,1,3:T(8,128)(2,1)S(1)} %get-tuple-element.25), kind=kOutput, calls=%fused_computation.15 | convolution fusion | flops 2097152 | bytes 2179072 | tf_op jit(solution)/shard_map/rhd,rthd->rht/dot_general | solution.py:139
  120.3 6.5 %fusion.37 = bf16[1024,128]{1,0:T(8,128)(2,1)} fusion(bf16[1024,4096]{1,0:T(8,128)(2,1)} %all-gather.3.cloned.1.call-done, bf16[4096,128]{1,0:T(8,128)(2,1)S(1)} %copy-done, f32[128]{0:T(128)S(1)} %copy-done.19), kind=kOutput, calls=%fused_computation.47 | convolution fusion | flops 1075052544 | bytes 9699840 | tf_op jit(solution)/shard_map/dot_general | solution.py:193
  126.8 2.9 %fusion.21 = f32[2,16,4,256]{3,1,2,0:T(8,128)S(1)} fusion(bf16[2,128,4,8,256]{4,3,2,1,0:T(8,128)(2,1)} %bitcast.288, f32[2,16,4,1024]{3,1,2,0:T(8,128)S(1)} %get-tuple-element.32, f32[2,16,4]{1,2,0:T(4,128)S(1)} %copy.245), kind=kOutput, calls=%fused_computation.25 | convolution fusion | flops 67371008 | bytes 4850176 | tf_op jit(solution)/shard_map/gqhj,gjhd->gqhd/dot_general | solution.py:157
  130.2 2.0 %fusion.6 = f32[32,4,1,256]{3,2,1,0:T(1,128)S(1)} fusion(bf16[32,4,4,8,256]{4,3,2,1,0:T(8,128)(2,1)} %bitcast.349, bf16[32,4,32,1]{2,0,1,3:T(8,128)(2,1)S(1)} %get-tuple-element.28), kind=kOutput, calls=%fused_computation.12 | convolution fusion | flops 2097152 | bytes 2236416 | tf_op jit(solution)/shard_map/rht,rthd->rhd/dot_general | solution.py:164
  132.7 1.5 reshape.376
  134.3 7.2 %all-to-all-start.2 = ((bf16[128,2,512]{2,1,0:T(2,128)(2,1)}), bf16[128,2,512]{2,1,0:T(2,128)(2,1)S(1)}, u32[]{:S(2)}, u32[]{:S(2)}) async-start(bf16[128,2,512]{2,1,0:T(2,128)(2,1)} %reshape.376), calls=%async_computation.2 | async-start | bytes 524288 | tf_op jit(solution)/shard_map/all_to_all | solution.py:178
  141.7 12.9 %all-to-all-done.2 = bf16[128,2,512]{2,1,0:T(2,128)(2,1)S(1)} async-done(((bf16[128,2,512]{2,1,0:T(2,128)(2,1)}), bf16[128,2,512]{2,1,0:T(2,128)(2,1)S(1)}, u32[]{:S(2)}, u32[]{:S(2)}) %all-to-all-start.2) | async-done | bytes 262176 | tf_op jit(solution)/shard_map/all_to_all | solution.py:178
  155.1 0.7 copy.252
  155.8 1.1 reshape.329
  156.9 2.5 %fusion.69 = f32[1024,1024]{1,0:T(8,128)S(1)} fusion(bf16[1024,512]{1,0:T(8,128)(2,1)} %all-gather.5.cloned.1.call-done, bf16[512,1024]{1,0:T(8,128)(2,1)S(1)} %bitcast_select_fusion), kind=kOutput, calls=%fused_computation.207 | convolution fusion | flops 1073741824 | bytes 6291456 | tf_op jit(solution)/shard_map/dot_general | solution.py:197
  159.4 0.8 bitcast_add_fusion
  160.8 2.3 %collective-permute-done.10 = bf16[1024,512]{1,0:T(8,128)(2,1)S(1)} collective-permute-done((bf16[1024,512]{1,0:T(8,128)(2,1)S(1)}, bf16[1024,512]{1,0:T(8,128)(2,1)S(1)}, u32[]{:S(2)}, u32[]{:S(2)}) %collective-permute-start.10) | collective-permute-done | bytes 1048608 | tf_op jit(solution)/shard_map/ppermute | solution.py:203
  163.1 1.4 add_convert_fusion
  164.5 4.5 %all-to-all-start.3 = ((bf16[32,32,512]{2,1,0:T(8,128)(2,1)}), bf16[32,32,512]{2,1,0:T(8,128)(2,1)S(1)}, u32[]{:S(2)}, u32[]{:S(2)}) async-start(bf16[32,32,512]{2,1,0:T(8,128)(2,1)} %bitcast.77), calls=%async_computation.3 | async-start | bytes 2097152 | tf_op jit(solution)/shard_map/all_to_all | solution.py:205
  169.0 17.0 %all-to-all-done.3 = bf16[32,32,512]{2,1,0:T(8,128)(2,1)S(1)} async-done(((bf16[32,32,512]{2,1,0:T(8,128)(2,1)}), bf16[32,32,512]{2,1,0:T(8,128)(2,1)S(1)}, u32[]{:S(2)}, u32[]{:S(2)}) %all-to-all-start.3) | async-done | bytes 1048608 | tf_op jit(solution)/shard_map/all_to_all | solution.py:205
  186.2 0.7 add_convert_fusion.3
  (153 shorter events, 22.5 us)
Async XLA Ops:
  6.5 113.8 %copy-start = (bf16[4096,128]{1,0:T(8,128)(2,1)S(1)}, bf16[4096,128]{1,0:T(8,128)(2,1)}, u32[]{:S(2)}) copy-start(bf16[4096,128]{1,0:T(8,128)(2,1)} %param.26) | copy-start | bytes 3145732
  6.5 11.4 %copy-start.10 = (bf16[4096]{0:T(1024)(128)(2,1)S(1)}, bf16[4096]{0:T(1024)(128)(2,1)}, u32[]{:S(2)}) copy-start(bf16[4096]{0:T(1024)(128)(2,1)} %param.16) | copy-start | bytes 24580
  6.5 11.4 %copy-start.11 = (bf16[4096]{0:T(1024)(128)(2,1)S(1)}, bf16[4096]{0:T(1024)(128)(2,1)}, u32[]{:S(2)}) copy-start(bf16[4096]{0:T(1024)(128)(2,1)} %param.17) | copy-start | bytes 24580
  6.5 113.8 %all-gather.3.cloned.1.call-start = ((), (), s32[]{:S(2)}) async-start(), calls=%async_computation.4 | async-start | bytes 8650752 | tf_op jit(solution)/shard_map/all_gather | solution.py:85
  6.5 6.6 %collective-permute-start = (bf16[32,1024]{1,0:T(8,128)(2,1)}, bf16[32,1024]{1,0:T(8,128)(2,1)S(1)}, u32[]{:S(2)}, u32[]{:S(2)}) collective-permute-start(bf16[32,1024]{1,0:T(8,128)(2,1)} %param.15), channel_id=1, source_target_pairs={{0,1},{1,2},{2,3},{3,0},{4,5},{5,6},{6,7},{7,4},{8,9},{9,10},{10,1... | collective-permute-start | bytes 196616 | tf_op jit(solution)/shard_map/ppermute | solution.py:55
  8.6 4.5 %collective-permute-start.2 = (bf16[32,1024]{1,0:T(8,128)(2,1)}, bf16[32,1024]{1,0:T(8,128)(2,1)S(1)}, u32[]{:S(2)}, u32[]{:S(2)}) collective-permute-start(bf16[32,1024]{1,0:T(8,128)(2,1)} %param.15), channel_id=1, source_target_pairs={{0,3},{1,0},{2,1},{3,2},{4,7},{5,4},{6,5},{7,6},{8,11},{9,8},{10,9... | collective-permute-start | bytes 196616 | tf_op jit(solution)/shard_map/ppermute | solution.py:55
  10.0 4.8 %collective-permute-start.1 = (bf16[32,1024]{1,0:T(8,128)(2,1)}, bf16[32,1024]{1,0:T(8,128)(2,1)S(1)}, u32[]{:S(2)}, u32[]{:S(2)}) collective-permute-start(bf16[32,1024]{1,0:T(8,128)(2,1)} %param.15), channel_id=1, source_target_pairs={{0,2},{1,3},{2,0},{3,1},{4,6},{5,7},{6,4},{7,5},{8,10},{9,11},{10,... | collective-permute-start | bytes 196616 | tf_op jit(solution)/shard_map/ppermute | solution.py:55
  11.7 4.6 %copy-start.14 = (s32[1024]{0:T(1024)}, s32[1024]{0:T(1024)S(1)}, u32[]{:S(2)}) copy-start(s32[1024]{0:T(1024)S(1)} %pad_clamp_fusion) | copy-start | bytes 12292
  13.1 4.9 %copy-start.13 = (pred[4]{0:T(512)(128)(4,1)}, pred[4]{0:T(512)(128)(4,1)S(1)}, u32[]{:S(2)}) copy-start(pred[4]{0:T(512)(128)(4,1)S(1)} %compare_and_fusion) | copy-start | bytes 16
  18.0 30.8 %copy-start.3 = (bf16[128,3,1024]{2,0,1:T(8,128)(2,1)S(1)}, bf16[128,3,1024]{2,0,1:T(8,128)(2,1)}, u32[]{:S(2)}) copy-start(bf16[128,3,1024]{2,0,1:T(8,128)(2,1)} %param.18) | copy-start | bytes 2359300
  38.2 24.3 %all-to-all-start = ((bf16[32,32,1,256]{3,1,2,0:T(8,128)(2,1)}), bf16[32,32,1,256]{3,1,2,0:T(8,128)(2,1)S(1)}, u32[]{:S(2)}, u32[]{:S(2)}) async-start(bf16[32,32,1,256]{3,1,2,0:T(8,128)(2,1)} %constant_dynamic-update-slice_fusion), calls=%async_computation | async-start | bytes 1048576 | tf_op jit(solution)/shard_map/all_to_all | solution.py:89
  48.9 1.8 collective-permute-start.6
  65.6 5.3 %copy-start.5 = (bf16[8,4,4096]{2,1,0:T(4,128)(2,1)S(1)}, bf16[8,4,4096]{2,1,0:T(4,128)(2,1)}, u32[]{:S(2)}) copy-start(bf16[8,4,4096]{2,1,0:T(4,128)(2,1)} %param.25) | copy-start | bytes 786436
  65.6 10.1 %copy-start.2 = (bf16[128,4096]{1,0:T(8,128)(2,1)S(1)}, bf16[128,4096]{1,0:T(8,128)(2,1)}, u32[]{:S(2)}) copy-start(bf16[128,4096]{1,0:T(8,128)(2,1)} %param.28) | copy-start | bytes 3145732
  65.6 43.7 %all-to-all-start.1 = ((bf16[32,32,3,512]{3,1,2,0:T(8,128)(2,1)}), bf16[32,32,3,512]{3,1,2,0:T(8,128)(2,1)}, u32[]{:S(2)}, u32[]{:S(2)}) async-start(bf16[32,32,3,512]{3,1,2,0:T(8,128)(2,1)} %copy.233), calls=%async_computation.1 | async-start | bytes 6291456 | tf_op jit(solution)/shard_map/all_to_all | solution.py:110
  70.8 86.1 %all-gather.5.cloned.1.call-start = ((), (), s32[]{:S(2)}) async-start(), calls=%async_computation.5 | async-start | bytes 1310720 | tf_op jit(solution)/shard_map/all_gather | solution.py:196
  71.8 8.4 %copy-start.18 = (s32[2]{0:T(128)S(1)}, s32[2]{0:T(128)}, u32[]{:S(2)}) copy-start(s32[2]{0:T(128)} %param.23) | copy-start | bytes 28
  71.8 8.5 %copy-start.17 = (s32[32]{0:T(128)S(1)}, s32[32]{0:T(128)}, u32[]{:S(2)}) copy-start(s32[32]{0:T(128)} %param.24) | copy-start | bytes 388
  72.5 12.6 %collective-permute-start.9 = (bf16[8,4,1024]{2,0,1:T(8,128)(2,1)}, bf16[8,4,1024]{2,0,1:T(8,128)(2,1)}, u32[]{:S(2)}, u32[]{:S(2)}) collective-permute-start(bf16[8,4,1024]{2,0,1:T(8,128)(2,1)} %bitcast.280), channel_id=1, source_target_pairs={{0,3},{1,0},{2,1},{3,2},{4,7},{5,4},{6,5},{7,6},{8,11},{9,8},{10,9... | collective-permute-start | bytes 196616 | tf_op jit(solution)/shard_map/ppermute | solution.py:43
  73.3 13.5 %collective-permute-start.7 = (bf16[8,4,1024]{2,0,1:T(8,128)(2,1)}, bf16[8,4,1024]{2,0,1:T(8,128)(2,1)}, u32[]{:S(2)}, u32[]{:S(2)}) collective-permute-start(bf16[8,4,1024]{2,0,1:T(8,128)(2,1)} %bitcast.282), channel_id=1, source_target_pairs={{0,1},{1,2},{2,3},{3,0},{4,5},{5,6},{6,7},{7,4},{8,9},{9,10},{10,1... | collective-permute-start | bytes 196616 | tf_op jit(solution)/shard_map/ppermute | solution.py:43
  75.4 11.4 %collective-permute-start.8 = (bf16[8,4,1024]{2,0,1:T(8,128)(2,1)}, bf16[8,4,1024]{2,0,1:T(8,128)(2,1)}, u32[]{:S(2)}, u32[]{:S(2)}) collective-permute-start(bf16[8,4,1024]{2,0,1:T(8,128)(2,1)} %bitcast.281), channel_id=1, source_target_pairs={{0,2},{1,3},{2,0},{3,1},{4,6},{5,7},{6,4},{7,5},{8,10},{9,11},{10,... | collective-permute-start | bytes 196616 | tf_op jit(solution)/shard_map/ppermute | solution.py:43
  76.6 13.2 %collective-permute-start.3 = (bf16[128,1024]{1,0:T(8,128)(2,1)S(1)}, bf16[128,1024]{1,0:T(8,128)(2,1)S(1)}, u32[]{:S(2)}, u32[]{:S(2)}) collective-permute-start(bf16[128,1024]{1,0:T(8,128)(2,1)S(1)} %bitcast.338), channel_id=1, source_target_pairs={{0,1},{1,2},{2,3},{3,0},{4,5},{5,6},{6,7},{7,4},{8,9},{9,10},{10,1... | collective-permute-start | bytes 786440 | tf_op jit(solution)/shard_map/ppermute | solution.py:43
  78.4 14.1 %collective-permute-start.4 = (bf16[128,1024]{1,0:T(8,128)(2,1)S(1)}, bf16[128,1024]{1,0:T(8,128)(2,1)}, u32[]{:S(2)}, u32[]{:S(2)}) collective-permute-start(bf16[128,1024]{1,0:T(8,128)(2,1)S(1)} %bitcast.339), channel_id=1, source_target_pairs={{0,2},{1,3},{2,0},{3,1},{4,6},{5,7},{6,4},{7,5},{8,10},{9,11},{10,... | collective-permute-start | bytes 786440 | tf_op jit(solution)/shard_map/ppermute | solution.py:43
  85.1 7.4 %collective-permute-start.5 = (bf16[128,1024]{1,0:T(8,128)(2,1)S(1)}, bf16[128,1024]{1,0:T(8,128)(2,1)S(1)}, u32[]{:S(2)}, u32[]{:S(2)}) collective-permute-start(bf16[128,1024]{1,0:T(8,128)(2,1)S(1)} %bitcast.340), channel_id=1, source_target_pairs={{0,3},{1,0},{2,1},{3,2},{4,7},{5,4},{6,5},{7,6},{8,11},{9,8},{10,9... | collective-permute-start | bytes 786440 | tf_op jit(solution)/shard_map/ppermute | solution.py:43
  92.5 0.7 copy-start.7
  109.4 3.2 %copy-start.8 = (f32[32,32]{0,1:T(8,128)S(1)}, f32[32,32]{0,1:T(8,128)}, u32[]{:S(2)}) copy-start(f32[32,32]{0,1:T(8,128)} %get-tuple-element.30) | copy-start | bytes 12292
  111.9 2.4 %copy-start.12 = (pred[2,1024]{1,0:T(4,128)(4,1)S(1)}, pred[2,1024]{1,0:T(4,128)(4,1)}, u32[]{:S(2)}) copy-start(pred[2,1024]{1,0:T(4,128)(4,1)} %iota_compare_fusion.1) | copy-start | bytes 6148
  114.3 5.8 %copy-start.9 = (pred[32,32]{1,0:T(8,128)(4,1)S(1)}, pred[32,32]{1,0:T(8,128)(4,1)}, u32[]{:S(2)}) copy-start(pred[32,32]{1,0:T(8,128)(4,1)} %iota_compare_fusion) | copy-start | bytes 3076
  114.3 6.0 %copy-start.19 = (f32[128]{0:T(128)S(1)}, f32[128]{0:T(128)}, u32[]{:S(2)}) copy-start(f32[128]{0:T(128)} %convert_element_type.110) | copy-start | bytes 1540
  130.2 11.2 %copy-start.16 = (pred[512]{0:T(512)(128)(4,1)S(1)}, pred[512]{0:T(512)(128)(4,1)}, u32[]{:S(2)}) copy-start(pred[512]{0:T(512)(128)(4,1)} %broadcast_bitcast_fusion) | copy-start | bytes 1540
  134.3 20.3 %all-to-all-start.2 = ((bf16[128,2,512]{2,1,0:T(2,128)(2,1)}), bf16[128,2,512]{2,1,0:T(2,128)(2,1)S(1)}, u32[]{:S(2)}, u32[]{:S(2)}) async-start(bf16[128,2,512]{2,1,0:T(2,128)(2,1)} %reshape.376), calls=%async_computation.2 | async-start | bytes 524288 | tf_op jit(solution)/shard_map/all_to_all | solution.py:178
  156.8 2.6 %copy-start.4 = (bf16[4,8,4,1024]{3,1,2,0:T(8,128)(2,1)S(1)}, bf16[4,8,4,1024]{3,1,2,0:T(8,128)(2,1)}, u32[]{:S(2)}) copy-start(bf16[4,8,4,1024]{3,1,2,0:T(8,128)(2,1)} %broadcast_select_fusion) | copy-start | bytes 786436
  160.2 26.7 %copy-start.1 = (bf16[4096,128]{1,0:T(8,128)(2,1)S(1)}, bf16[4096,128]{1,0:T(8,128)(2,1)}, u32[]{:S(2)}) copy-start(bf16[4096,128]{1,0:T(8,128)(2,1)} %param.26) | copy-start | bytes 3145732
  160.4 8.6 %copy-start.15 = (bf16[1024]{0:T(1024)(128)(2,1)S(1)}, bf16[1024]{0:T(1024)(128)(2,1)}, u32[]{:S(2)}) copy-start(bf16[1024]{0:T(1024)(128)(2,1)} %param.29) | copy-start | bytes 6148
  160.4 25.8 %copy-start.6 = (bf16[32,1024]{1,0:T(8,128)(2,1)S(1)}, bf16[32,1024]{1,0:T(8,128)(2,1)}, u32[]{:S(2)}) copy-start(bf16[32,1024]{1,0:T(8,128)(2,1)} %param.15) | copy-start | bytes 196612
  160.4 2.7 %collective-permute-start.10 = (bf16[1024,512]{1,0:T(8,128)(2,1)S(1)}, bf16[1024,512]{1,0:T(8,128)(2,1)S(1)}, u32[]{:S(2)}, u32[]{:S(2)}) collective-permute-start(bf16[1024,512]{1,0:T(8,128)(2,1)S(1)} %dynamic-slice_convert_fusion), channel_id=1, source_target_pairs={{0,4},{4,0},{8,12},{12,8},{16,20},{20,16},{24,28},{28,24},{32,36},... | collective-permute-start | bytes 3145736 | tf_op jit(solution)/shard_map/ppermute | solution.py:203
  164.5 21.5 %all-to-all-start.3 = ((bf16[32,32,512]{2,1,0:T(8,128)(2,1)}), bf16[32,32,512]{2,1,0:T(8,128)(2,1)S(1)}, u32[]{:S(2)}, u32[]{:S(2)}) async-start(bf16[32,32,512]{2,1,0:T(8,128)(2,1)} %bitcast.77), calls=%async_computation.3 | async-start | bytes 2097152 | tf_op jit(solution)/shard_map/all_to_all | solution.py:205
Sparse Core Ops, SparseCore 0:
  18.0 62.6 all-gather.2
  126.9 24.6 all-gather.4
